TPU v7x, 32 devices: a whole 2x2x4 slice. The times are simulated.
32 devices in a mesh: energy: 4 (over z), atom: 8 (over y, x, core).
Axes of the slice: x: 2, y: 2, z: 4, core: 2. Of those that a mesh axis runs over, the one named last changes fastest.
Arguments:
- t_mats: bfloat16 [4, 16, 2048], P('energy', 'atom'), may hold values from -0.75 to 0.75
- struct_table: bfloat16 [4, 64, 2048], P('energy'), may hold values from -0.359375 to 0.359375
- zone_atoms: int32 [16, 64], P('atom'), may hold values from 0 to 15, as said below
- zone_size: int32 [16], P('atom'), may hold values from 32 to 64
- pair_index: int32 [16, 384], P('atom'), may hold values from 0 to 63
- zone_link: int32 [16, 384], P('atom'), may hold values from 0 to 63
- weights: float32 [4, 2], P('energy'), may hold values from -1 to 1
Outputs:
- green: float32 [16, 2048], P('atom')
Inputs may be any that keep to these rules, and one draw needn't show every extreme that they name: Atom g is owned by index g // 2 of the atom axis; zone_atoms[g, 0] is g; the owner of every member of atom g's zone lies -4 to 3 steps from g's owner along the atom axis, counted around the axis, and both extreme offsets occur in every zone; members may repeat (periodic images).
All inputs are finite; a program needn't handle non-finite values.
Results may differ from a plain program's by a relative error of at most 0.003.
Values may be sent and summed in bfloat16 or wider, within the bound.
No kernel may reach another device: no remote copies, remote signals or barrier semaphores. Data moves between devices by JAX's collectives and lax.ppermute only.
A program may use at most 128 MiB of HBM per device.

v0:
```python
import jax
import jax.numpy as jnp
from jax import lax
from jax.sharding import PartitionSpec as P

L = 32
Z = 64
NB = 6
ITERS = 3


def real_form(block):
    parts = block.reshape(block.shape[:-1] + (2, L, L))
    real_part = parts[..., 0, :, :]
    imag_part = parts[..., 1, :, :]
    top_rows = jnp.concatenate([real_part, -imag_part], axis=-1)
    bottom_rows = jnp.concatenate([imag_part, real_part], axis=-1)
    return jnp.concatenate([top_rows, bottom_rows], axis=-2)


def scatter_terms(couplings, gathered, pattern):
    products = jnp.einsum(pattern, couplings, gathered, preferred_element_type=jnp.float32)
    real_part = products[..., 0, 0, :, :] - products[..., 1, 1, :, :]
    imag_part = products[..., 1, 0, :, :] + products[..., 0, 1, :, :]
    return jnp.concatenate([real_part, imag_part], axis=-2)


def take_links(column_parts, link_rows):
    return jax.vmap(
        lambda member_col, member_links: member_col[:, member_links], in_axes=(1, 0), out_axes=1
    )(column_parts, link_rows)


def solve_zones(zone_block, couplings_flat, links):
    e_dev, a_dev = (zone_block.shape[0], zone_block.shape[1])
    t_real = real_form(zone_block)
    couplings = couplings_flat.reshape(e_dev, a_dev, Z, NB, 2, L, L)
    start_block = t_real[:, :, 0, :, :L].astype(jnp.float32)
    start = jnp.zeros((e_dev, a_dev, Z, 2 * L, L), jnp.float32).at[:, :, 0].set(start_block)
    column = start
    for repeat in range(ITERS - 1):
        column_parts = column.astype(jnp.bfloat16).reshape(e_dev, a_dev, Z, 2, L, L)
        gathered = take_links(column_parts, links).reshape(e_dev, a_dev, Z, NB, 2, L, L)
        coupled = scatter_terms(couplings, gathered, "eganpij,eganqjk->egapqik").astype(
            jnp.bfloat16
        )
        column = (
            jnp.einsum("egaij,egajk->egaik", t_real, coupled, preferred_element_type=jnp.float32)
            + start
        )
    column_parts = column.astype(jnp.bfloat16).reshape(e_dev, a_dev, Z, 2, L, L)
    gathered = take_links(column_parts, links[:, :NB])
    coupled = scatter_terms(couplings[:, :, 0], gathered, "egnpij,egnqjk->egpqik").astype(
        jnp.bfloat16
    )
    return (
        jnp.einsum("egij,egjk->egik", t_real[:, :, 0], coupled, preferred_element_type=jnp.float32)
        + start_block
    )


def body(t_mats, struct_table, zone_atoms, zone_size, pair_index, zone_link, weights):
    e_dev, a_dev, block_flat = t_mats.shape
    window = lax.all_gather(t_mats, "atom", axis=1, tiled=True)
    present = jnp.arange(Z, dtype=jnp.int32)[None, :] < zone_size[:, None]
    zone_block = jnp.where(
        present[None, :, :, None], window[:, zone_atoms], jnp.zeros((), jnp.bfloat16)
    )
    couplings_flat = struct_table[:, pair_index]
    diagonal = solve_zones(zone_block, couplings_flat, zone_link)
    real_rows = diagonal[:, :, :L, :].reshape(e_dev, a_dev, L * L)
    imag_rows = diagonal[:, :, L:, :].reshape(e_dev, a_dev, L * L)
    w_real = weights[:, 0][:, None, None]
    w_imag = weights[:, 1][:, None, None]
    green_real = jnp.sum(w_real * real_rows - w_imag * imag_rows, axis=0)
    green_imag = jnp.sum(w_real * imag_rows + w_imag * real_rows, axis=0)
    local_green = jnp.concatenate([green_real, green_imag], axis=-1)
    return lax.psum(local_green, "energy")


def solution(mesh):
    return jax.shard_map(
        body,
        mesh=mesh,
        in_specs=(
            P("energy", "atom", None),
            P("energy", None, None),
            P("atom", None),
            P("atom"),
            P("atom", None),
            P("atom", None),
            P("energy", None),
        ),
        out_specs=P("atom", None),
        check_vma=False,
    )
```

profile of v0, /device:TPU:0, one launch (start us, length us, event | category | flops | bytes accessed | tf_op | source)
XLA Modules:
  0.0 153.0 jit_solution(8475652753170242469)
XLA Ops:
  0.0 0.8 copy.91
  0.8 10.7 %all_gather.3 = bf16[1,16,2048]{2,0,1:T(2,128)(2,1)S(1)} all-gather(bf16[1,2,2048]{2,0,1:T(2,128)(2,1)S(1)} %copy.91), channel_id=1, replica_groups=mesh['energy'=4,'atom'=8] {'atom'}, dimensions={1}, use_global_device_ids=true | all-gather | bytes 73728 | tf_op jit(solution)/shard_map/all_gather | solution.py:64
  11.5 0.7 compare_select_fusion.3
  12.2 0.1 reshape.287
  12.3 0.9 gather_fusion
  13.2 0.3 copy.92
  13.5 0.4 gather.18
  13.9 2.0 %copy.93 = bf16[1,2,64,2,32,32]{5,4,2,1,3,0:T(8,128)(2,1)S(1)} copy(bf16[1,2,64,2,32,32]{2,1,5,4,3,0:T(2,128)(2,1)S(1)} %gather.18) | data formatting | bytes 1048576 | tf_op jit(solution)/shard_map/gather | solution.py:67
  15.9 0.1 iota_compare_fusion
  15.9 0.2 broadcast_select_fusion
  16.2 0.4 slice_bitcast_fusion.4
  16.6 0.1 fusion.57
  16.7 1.2 maximum_maximum_fusion
  17.9 0.5 scatter.9
  18.4 0.8 copy-done.4
  19.3 9.2 %gather_fusion.2 = bf16[768,2,32,32]{3,2,1,0:T(8,128)(2,1)} fusion(bf16[2,64,2,32,32]{4,3,2,1,0:T(8,128)(2,1)S(1)} %bitcast.153, s32[768]{0:T(1024)S(1)} %reshape.305), kind=kCustom, calls=%fused_computation.2 | custom fusion | bytes 6297600 | tf_op jit(solution)/shard_map/vmap()/gather | solution.py:30
  28.5 3.4 %gather_fusion.1 = bf16[768,2048]{1,0:T(8,128)(2,1)S(1)} fusion(bf16[64,2048]{1,0:T(8,128)(2,1)S(1)} %bitcast.151, s32[1024]{0:T(1024)S(1)} %pad_clamp_fusion), kind=kCustom, calls=%fused_computation.1 | custom fusion | bytes 6294528 | tf_op jit(solution)/shard_map/gather | solution.py:69
  31.9 11.8 %reshape.277 = bf16[2,64,6,2,32,32]{5,4,3,2,1,0:T(8,128)(2,1)} reshape(bf16[768,2048]{1,0:T(8,128)(2,1)S(1)} %gather_fusion.1) | data formatting | bytes 6291456 | tf_op jit(solution)/shard_map/reshape.48
  43.7 17.2 %fusion.6 = f32[1,2,64,2,2,32,32]{5,6,3,4,2,1,0:T(8,128)} fusion(bf16[2,64,6,2,32,32,1]{5,4,3,2,1,0,6:T(8,128)(2,1)} %bitcast.155, bf16[2,64,6,2,32,32]{5,4,3,2,1,0:T(8,128)(2,1)} %reshape.277), kind=kOutput, calls=%fused_computation.11 | convolution fusion | flops 201326592 | bytes 8388608 | tf_op jit(solution)/shard_map/eganpij,eganqjk->egapqik/dot_general | solution.py:22
  60.9 2.7 %fusion.27 = bf16[2,64,32,32]{2,3,1,0:T(8,128)(2,1)S(1)} fusion(f32[1,2,64,2,2,32,32]{5,6,3,4,2,1,0:T(8,128)} %fusion.6), kind=kLoop, calls=%fused_computation.34 | loop fusion | flops 262144 | bytes 1310720 | tf_op jit(solution)/shard_map/sub | solution.py:23
  63.7 2.9 %fusion.28 = bf16[2,64,32,32]{2,3,1,0:T(8,128)(2,1)S(1)} fusion(f32[1,2,64,2,2,32,32]{5,6,3,4,2,1,0:T(8,128)} %fusion.6), kind=kLoop, calls=%fused_computation.35 | loop fusion | flops 262144 | bytes 1310720 | tf_op jit(solution)/shard_map/add | solution.py:24
  66.6 1.3 fusion.24
  67.9 1.3 copy-done.7
  69.2 0.1 copy.140
  69.3 0.1 copy.99
  69.4 0.6 constant_dynamic-update-slice_fusion.1
  70.0 1.8 %convert_element_type.37 = bf16[1,2,64,64,32]{3,4,2,1,0:T(8,128)(2,1)S(1)} convert(f32[1,2,64,64,32]{3,4,2,1,0:T(8,128)} %constant_dynamic-update-slice_fusion.1) | non-fusion elementwise | flops 262144 | bytes 1572864 | tf_op jit(solution)/shard_map/convert_element_type | solution.py:42
  71.8 1.2 copy.129
  73.0 9.4 %gather_fusion.3 = bf16[768,2,32,32]{3,2,1,0:T(8,128)(2,1)} fusion(bf16[2,64,2,32,32]{4,3,2,1,0:T(8,128)(2,1)S(1)} %bitcast.154, s32[768]{0:T(1024)S(1)} %reshape.305), kind=kCustom, calls=%fused_computation.3 | custom fusion | bytes 6297600 | tf_op jit(solution)/shard_map/vmap()/gather | solution.py:30
  82.4 17.2 %fusion.11 = f32[1,2,64,2,2,32,32]{5,6,3,4,2,1,0:T(8,128)} fusion(bf16[2,64,6,2,32,32,1]{5,4,3,2,1,0,6:T(8,128)(2,1)} %bitcast.156, bf16[2,64,6,2,32,32]{5,4,3,2,1,0:T(8,128)(2,1)} %reshape.277), kind=kOutput, calls=%fused_computation.12 | convolution fusion | flops 201326592 | bytes 8388608 | tf_op jit(solution)/shard_map/eganpij,eganqjk->egapqik/dot_general | solution.py:22
  99.6 2.7 %fusion.29 = bf16[2,64,32,32]{2,3,1,0:T(8,128)(2,1)S(1)} fusion(f32[1,2,64,2,2,32,32]{5,6,3,4,2,1,0:T(8,128)} %fusion.11), kind=kLoop, calls=%fused_computation.36 | loop fusion | flops 262144 | bytes 1310720 | tf_op jit(solution)/shard_map/sub | solution.py:23
  102.3 2.9 %fusion.30 = bf16[2,64,32,32]{2,3,1,0:T(8,128)(2,1)S(1)} fusion(f32[1,2,64,2,2,32,32]{5,6,3,4,2,1,0:T(8,128)} %fusion.11), kind=kLoop, calls=%fused_computation.37 | loop fusion | flops 262144 | bytes 1310720 | tf_op jit(solution)/shard_map/add | solution.py:24
  105.2 1.3 fusion.22
  106.5 1.3 copy-done.8
  107.8 0.1 copy.143
  108.0 0.6 constant_dynamic-update-slice_fusion
  108.6 2.8 %convert_element_type.38 = bf16[1,2,64,64,32]{3,4,2,1,0:T(8,128)(2,1)} convert(f32[1,2,64,64,32]{3,4,2,1,0:T(8,128)} %constant_dynamic-update-slice_fusion) | non-fusion elementwise | flops 262144 | bytes 1572864 | tf_op jit(solution)/shard_map/convert_element_type | solution.py:51
  111.4 2.9 %copy.134 = bf16[1,2,64,64,32]{4,3,2,1,0:T(8,128)(2,1)} copy(bf16[1,2,64,64,32]{3,4,2,1,0:T(8,128)(2,1)} %convert_element_type.38) | data formatting | bytes 1048576 | tf_op jit(solution)/shard_map/vmap()/transpose;reshape | solution.py:30
  114.3 0.1 reshape.321
  114.4 2.9 %gather_fusion.4 = bf16[12,2,32,32]{3,2,1,0:T(8,128)(2,1)} fusion(bf16[2,64,2,32,32]{4,3,2,1,0:T(8,128)(2,1)} %bitcast.159, s32[12]{0:T(128)S(1)} %reshape.321), kind=kCustom, calls=%fused_computation.4 | custom fusion | bytes 98400 | tf_op jit(solution)/shard_map/vmap()/gather | solution.py:30
  117.4 11.6 %reshape.280 = bf16[1,2,64,6,2,32,32]{6,5,4,3,2,1,0:T(8,128)(2,1)} reshape(bf16[768,2048]{1,0:T(8,128)(2,1)S(1)} %copy-done.3) | data formatting | bytes 6291456 | tf_op jit(solution)/shard_map/reshape | solution.py:37
  129.0 1.3 convolution_bitcast_fusion
  130.3 1.0 fusion.26
  131.4 0.6 fusion.58
  132.0 1.2 multiply_subtract_fusion
  133.2 0.1 add.92
  133.3 0.1 sub.43
  133.4 19.6 %psum.7 = f32[2,2048]{1,0:T(2,128)} all-reduce(f32[2,2048]{1,0:T(2,128)S(1)} %pad_maximum_fusion), channel_id=1, replica_groups=mesh['energy'=4,'atom'=8] {'energy'}, use_global_device_ids=true, to_apply=%region_0.1 | all-reduce | flops 4096 | bytes 32768 | tf_op jit(solution)/shard_map/psum | solution.py:78
  (40 shorter events, 0.3 us)
Async XLA Ops:
  0.0 28.5 %copy-start = (bf16[1,64,2048]{2,1,0:T(8,128)(2,1)S(1)}, bf16[1,64,2048]{2,1,0:T(8,128)(2,1)}, u32[]{:S(2)}) copy-start(bf16[1,64,2048]{2,1,0:T(8,128)(2,1)} %param.10) | copy-start | bytes 786436
  13.5 2.4 %copy-start.12 = (s32[2]{0:T(128)S(1)}, s32[2]{0:T(128)}, u32[]{:S(2)}) copy-start(s32[2]{0:T(128)} %param.12) | copy-start | bytes 28
  17.9 1.4 copy-start.4
  17.9 1.4 copy-start.9
  19.3 9.2 %copy-start.10 = (s32[2,384]{1,0:T(2,128)S(1)}, s32[2,384]{1,0:T(2,128)}, u32[]{:S(2)}) copy-start(s32[2,384]{1,0:T(2,128)} %param.13) | copy-start | bytes 9220
  31.9 11.8 %copy-start.2 = (bf16[768,2048]{1,0:T(8,128)(2,1)}, bf16[768,2048]{1,0:T(8,128)(2,1)S(1)}, u32[]{:S(2)}) copy-start(bf16[768,2048]{1,0:T(8,128)(2,1)S(1)} %gather_fusion.1) | copy-start | bytes 9437188
  63.7 2.9 %copy-start.5 = (bf16[1,2,64,64,64]{4,3,2,1,0:T(8,128)(2,1)S(1)}, bf16[1,2,64,64,64]{4,3,2,1,0:T(8,128)(2,1)}, u32[]{:S(2)}) copy-start(bf16[1,2,64,64,64]{4,3,2,1,0:T(8,128)(2,1)} %copy-done.4) | copy-start | bytes 3145732
  67.9 1.3 copy-start.7
  102.3 2.9 %copy-start.6 = (bf16[1,2,64,64,64]{4,3,2,1,0:T(8,128)(2,1)S(1)}, bf16[1,2,64,64,64]{4,3,2,1,0:T(8,128)(2,1)}, u32[]{:S(2)}) copy-start(bf16[1,2,64,64,64]{4,3,2,1,0:T(8,128)(2,1)} %copy-done.4) | copy-start | bytes 3145732
  106.5 1.3 copy-start.8
  111.4 5.9 %copy-start.3 = (bf16[768,2048]{1,0:T(8,128)(2,1)S(1)}, bf16[768,2048]{1,0:T(8,128)(2,1)}, u32[]{:S(2)}) copy-start(bf16[768,2048]{1,0:T(8,128)(2,1)} %copy-done.2) | copy-start | bytes 9437188
  117.3 14.0 %copy-start.11 = (f32[1,2]{1,0:T(1,128)S(1)}, f32[1,2]{1,0:T(1,128)}, u32[]{:S(2)}) copy-start(f32[1,2]{1,0:T(1,128)} %param.15) | copy-start | bytes 28
  117.3 35.6 %copy-start.1 = (bf16[1,64,2048]{2,1,0:T(8,128)(2,1)S(1)}, bf16[1,64,2048]{2,1,0:T(8,128)(2,1)}, u32[]{:S(2)}) copy-start(bf16[1,64,2048]{2,1,0:T(8,128)(2,1)} %param.10) | copy-start | bytes 786436
where the time goes:
time: 153 us
  local copies, waits for them, and re-layouts  63.7 us (42%)
  matrix products  39.3 us (26%)
  blocking collectives  30.3 us (20%)
  other arithmetic  19.4 us (13%)
    dot_general x3, matrix products, scatter_terms(): jnp.einsum(pattern, couplings, gathered, preferred_element_type=jnp.float32)  35.7 us
    gather x5, local copies, waits for them, and re-layouts, take_links(): member_col[:, member_links]  21.5 us
    psum x1, blocking collectives, body(): return lax.psum(local_green, 'energy')  19.6 us
    another operation x3, local copies, waits for them, and re-layouts  11.8 us
    reshape x1, local copies, waits for them, and re-layouts, solve_zones(): couplings = couplings_flat.reshape(e_dev, a_dev, Z, NB, 2, L, L)  11.6 us
    all_gather x1, blocking collectives, body(): window = lax.all_gather(t_mats, 'atom', axis=1, tiled=True)  10.7 us
    add x3, other arithmetic, scatter_terms(): imag_part = products[..., 1, 0, :, :] + products[..., 0, 1, :, :]  5.8 us
    sub x3, other arithmetic, scatter_terms(): real_part = products[..., 0, 0, :, :] - products[..., 1, 1, :, :]  5.49 us

commit v1 on v0

--- a/solution.py
+++ b/solution.py
@@ -75,7 +75,7 @@
     green_real = jnp.sum(w_real * real_rows - w_imag * imag_rows, axis=0)
     green_imag = jnp.sum(w_real * imag_rows + w_imag * real_rows, axis=0)
     local_green = jnp.concatenate([green_real, green_imag], axis=-1)
-    return lax.psum(local_green, "energy")
+    return jnp.sum(lax.all_gather(local_green, "energy"), axis=0)
 
 
 def solution(mesh):

time: 153 us -> 148 us (0.967)
  blocking collectives: 30.3 us -> 24 us
    psum x1 -> x0, blocking collectives: 19.6 us -> none  [body(): return lax.psum(local_green, 'energy')]
    all_gather x0 -> x1, blocking collectives: none -> 13.3 us  [body(): return jnp.sum(lax.all_gather(local_green, 'energy'), axis=0)]
where the time goes in v1:
time: 148 us; the launch traced here: 147 us
  local copies, waits for them, and re-layouts  63.7 us (43%)
  matrix products  39.3 us (27%)
  blocking collectives  24 us (16%)
  other arithmetic  20.1 us (14%)
    dot_general x3, matrix products, scatter_terms(): jnp.einsum(pattern, couplings, gathered, preferred_element_type=jnp.float32)  35.7 us
    gather x5, local copies, waits for them, and re-layouts, take_links(): member_col[:, member_links]  21.5 us
    all_gather x1, blocking collectives, body(): return jnp.sum(lax.all_gather(local_green, 'energy'), axis=0)  13.3 us
    another operation x3, local copies, waits for them, and re-layouts  11.8 us
    reshape x1, local copies, waits for them, and re-layouts, solve_zones(): couplings = couplings_flat.reshape(e_dev, a_dev, Z, NB, 2, L, L)  11.6 us
    all_gather x1, blocking collectives, body(): window = lax.all_gather(t_mats, 'atom', axis=1, tiled=True)  10.7 us
    add x3, other arithmetic, scatter_terms(): imag_part = products[..., 1, 0, :, :] + products[..., 0, 1, :, :]  5.8 us
    sub x3, other arithmetic, scatter_terms(): real_part = products[..., 0, 0, :, :] - products[..., 1, 1, :, :]  5.49 us

profile of v1, /device:TPU:0, one launch (start us, length us, event | category | flops | bytes accessed | tf_op | source)
XLA Modules:
  0.0 147.4 jit_solution(8224166855393187632)
XLA Ops:
  0.0 0.8 copy.91
  0.8 10.7 %all_gather.9 = bf16[1,16,2048]{2,0,1:T(2,128)(2,1)S(1)} all-gather(bf16[1,2,2048]{2,0,1:T(2,128)(2,1)S(1)} %copy.91), channel_id=1, replica_groups=mesh['energy'=4,'atom'=8] {'atom'}, dimensions={1}, use_global_device_ids=true | all-gather | bytes 73728 | tf_op jit(solution)/shard_map/all_gather | solution.py:64
  11.5 0.7 compare_select_fusion.3
  12.2 0.1 reshape.287
  12.3 0.9 gather_fusion
  13.2 0.3 copy.92
  13.5 0.4 gather.18
  13.9 2.0 %copy.93 = bf16[1,2,64,2,32,32]{5,4,2,1,3,0:T(8,128)(2,1)S(1)} copy(bf16[1,2,64,2,32,32]{2,1,5,4,3,0:T(2,128)(2,1)S(1)} %gather.18) | data formatting | bytes 1048576 | tf_op jit(solution)/shard_map/gather | solution.py:67
  15.9 0.1 iota_compare_fusion
  15.9 0.2 broadcast_select_fusion
  16.2 0.4 slice_bitcast_fusion.4
  16.6 0.1 fusion.57
  16.7 1.2 maximum_maximum_fusion
  17.9 0.5 scatter.9
  18.4 0.8 copy-done.4
  19.3 9.2 %gather_fusion.2 = bf16[768,2,32,32]{3,2,1,0:T(8,128)(2,1)} fusion(bf16[2,64,2,32,32]{4,3,2,1,0:T(8,128)(2,1)S(1)} %bitcast.155, s32[768]{0:T(1024)S(1)} %reshape.305), kind=kCustom, calls=%fused_computation.2 | custom fusion | bytes 6297600 | tf_op jit(solution)/shard_map/vmap()/gather | solution.py:30
  28.5 3.4 %gather_fusion.1 = bf16[768,2048]{1,0:T(8,128)(2,1)S(1)} fusion(bf16[64,2048]{1,0:T(8,128)(2,1)S(1)} %bitcast.153, s32[1024]{0:T(1024)S(1)} %pad_clamp_fusion), kind=kCustom, calls=%fused_computation.1 | custom fusion | bytes 6294528 | tf_op jit(solution)/shard_map/gather | solution.py:69
  31.9 11.8 %reshape.277 = bf16[2,64,6,2,32,32]{5,4,3,2,1,0:T(8,128)(2,1)} reshape(bf16[768,2048]{1,0:T(8,128)(2,1)S(1)} %gather_fusion.1) | data formatting | bytes 6291456 | tf_op jit(solution)/shard_map/reshape.48
  43.7 17.2 %fusion.6 = f32[1,2,64,2,2,32,32]{5,6,3,4,2,1,0:T(8,128)} fusion(bf16[2,64,6,2,32,32,1]{5,4,3,2,1,0,6:T(8,128)(2,1)} %bitcast.157, bf16[2,64,6,2,32,32]{5,4,3,2,1,0:T(8,128)(2,1)} %reshape.277), kind=kOutput, calls=%fused_computation.11 | convolution fusion | flops 201326592 | bytes 8388608 | tf_op jit(solution)/shard_map/eganpij,eganqjk->egapqik/dot_general | solution.py:22
  60.9 2.7 %fusion.27 = bf16[2,64,32,32]{2,3,1,0:T(8,128)(2,1)S(1)} fusion(f32[1,2,64,2,2,32,32]{5,6,3,4,2,1,0:T(8,128)} %fusion.6), kind=kLoop, calls=%fused_computation.34 | loop fusion | flops 262144 | bytes 1310720 | tf_op jit(solution)/shard_map/sub | solution.py:23
  63.7 2.9 %fusion.28 = bf16[2,64,32,32]{2,3,1,0:T(8,128)(2,1)S(1)} fusion(f32[1,2,64,2,2,32,32]{5,6,3,4,2,1,0:T(8,128)} %fusion.6), kind=kLoop, calls=%fused_computation.35 | loop fusion | flops 262144 | bytes 1310720 | tf_op jit(solution)/shard_map/add | solution.py:24
  66.6 1.3 fusion.24
  67.9 1.3 copy-done.7
  69.2 0.1 copy.140
  69.4 0.6 constant_dynamic-update-slice_fusion.1
  70.0 1.8 %convert_element_type.37 = bf16[1,2,64,64,32]{3,4,2,1,0:T(8,128)(2,1)S(1)} convert(f32[1,2,64,64,32]{3,4,2,1,0:T(8,128)} %constant_dynamic-update-slice_fusion.1) | non-fusion elementwise | flops 262144 | bytes 1572864 | tf_op jit(solution)/shard_map/convert_element_type | solution.py:42
  71.8 1.2 copy.129
  73.0 9.4 %gather_fusion.3 = bf16[768,2,32,32]{3,2,1,0:T(8,128)(2,1)} fusion(bf16[2,64,2,32,32]{4,3,2,1,0:T(8,128)(2,1)S(1)} %bitcast.156, s32[768]{0:T(1024)S(1)} %reshape.305), kind=kCustom, calls=%fused_computation.3 | custom fusion | bytes 6297600 | tf_op jit(solution)/shard_map/vmap()/gather | solution.py:30
  82.4 17.2 %fusion.11 = f32[1,2,64,2,2,32,32]{5,6,3,4,2,1,0:T(8,128)} fusion(bf16[2,64,6,2,32,32,1]{5,4,3,2,1,0,6:T(8,128)(2,1)} %bitcast.158, bf16[2,64,6,2,32,32]{5,4,3,2,1,0:T(8,128)(2,1)} %reshape.277), kind=kOutput, calls=%fused_computation.12 | convolution fusion | flops 201326592 | bytes 8388608 | tf_op jit(solution)/shard_map/eganpij,eganqjk->egapqik/dot_general | solution.py:22
  99.6 2.7 %fusion.29 = bf16[2,64,32,32]{2,3,1,0:T(8,128)(2,1)S(1)} fusion(f32[1,2,64,2,2,32,32]{5,6,3,4,2,1,0:T(8,128)} %fusion.11), kind=kLoop, calls=%fused_computation.36 | loop fusion | flops 262144 | bytes 1310720 | tf_op jit(solution)/shard_map/sub | solution.py:23
  102.3 2.9 %fusion.30 = bf16[2,64,32,32]{2,3,1,0:T(8,128)(2,1)S(1)} fusion(f32[1,2,64,2,2,32,32]{5,6,3,4,2,1,0:T(8,128)} %fusion.11), kind=kLoop, calls=%fused_computation.37 | loop fusion | flops 262144 | bytes 1310720 | tf_op jit(solution)/shard_map/add | solution.py:24
  105.2 1.3 fusion.22
  106.5 1.3 copy-done.8
  107.8 0.1 copy.143
  108.0 0.6 constant_dynamic-update-slice_fusion
  108.6 2.8 %convert_element_type.38 = bf16[1,2,64,64,32]{3,4,2,1,0:T(8,128)(2,1)} convert(f32[1,2,64,64,32]{3,4,2,1,0:T(8,128)} %constant_dynamic-update-slice_fusion) | non-fusion elementwise | flops 262144 | bytes 1572864 | tf_op jit(solution)/shard_map/convert_element_type | solution.py:51
  111.4 2.9 %copy.134 = bf16[1,2,64,64,32]{4,3,2,1,0:T(8,128)(2,1)} copy(bf16[1,2,64,64,32]{3,4,2,1,0:T(8,128)(2,1)} %convert_element_type.38) | data formatting | bytes 1048576 | tf_op jit(solution)/shard_map/vmap()/transpose;reshape | solution.py:30
  114.3 0.1 reshape.321
  114.4 2.9 %gather_fusion.4 = bf16[12,2,32,32]{3,2,1,0:T(8,128)(2,1)} fusion(bf16[2,64,2,32,32]{4,3,2,1,0:T(8,128)(2,1)} %bitcast.161, s32[12]{0:T(128)S(1)} %reshape.321), kind=kCustom, calls=%fused_computation.4 | custom fusion | bytes 98400 | tf_op jit(solution)/shard_map/vmap()/gather | solution.py:30
  117.4 11.6 %reshape.280 = bf16[1,2,64,6,2,32,32]{6,5,4,3,2,1,0:T(8,128)(2,1)} reshape(bf16[768,2048]{1,0:T(8,128)(2,1)S(1)} %copy-done.3) | data formatting | bytes 6291456 | tf_op jit(solution)/shard_map/reshape | solution.py:37
  129.0 1.3 convolution_bitcast_fusion
  130.3 1.0 fusion.26
  131.4 0.6 fusion.58
  132.0 1.2 multiply_subtract_fusion
  133.2 0.1 add.90
  133.3 0.1 sub.43
  133.4 13.3 %all-gather.1 = f32[4,2,2048]{2,1,0:T(2,128)S(1)} all-gather(f32[1,2,2048]{2,1,0:T(2,128)S(1)} %maximum_bitcast_fusion), channel_id=2, replica_groups=mesh['energy'=4,'atom'=8] {'energy'}, dimensions={0}, use_global_device_ids=true | all-gather | bytes 81920 | tf_op jit(solution)/shard_map/all_gather | solution.py:78
  146.7 0.6 reduce_sum.8
  (41 shorter events, 0.3 us)
Async XLA Ops:
  0.0 28.5 %copy-start = (bf16[1,64,2048]{2,1,0:T(8,128)(2,1)S(1)}, bf16[1,64,2048]{2,1,0:T(8,128)(2,1)}, u32[]{:S(2)}) copy-start(bf16[1,64,2048]{2,1,0:T(8,128)(2,1)} %param.10) | copy-start | bytes 786436
  13.5 2.4 %copy-start.12 = (s32[2]{0:T(128)S(1)}, s32[2]{0:T(128)}, u32[]{:S(2)}) copy-start(s32[2]{0:T(128)} %param.12) | copy-start | bytes 28
  17.9 1.4 copy-start.4
  17.9 1.4 copy-start.9
  19.3 9.2 %copy-start.10 = (s32[2,384]{1,0:T(2,128)S(1)}, s32[2,384]{1,0:T(2,128)}, u32[]{:S(2)}) copy-start(s32[2,384]{1,0:T(2,128)} %param.13) | copy-start | bytes 9220
  31.9 11.8 %copy-start.2 = (bf16[768,2048]{1,0:T(8,128)(2,1)}, bf16[768,2048]{1,0:T(8,128)(2,1)S(1)}, u32[]{:S(2)}) copy-start(bf16[768,2048]{1,0:T(8,128)(2,1)S(1)} %gather_fusion.1) | copy-start | bytes 9437188
  63.7 2.9 %copy-start.5 = (bf16[1,2,64,64,64]{4,3,2,1,0:T(8,128)(2,1)S(1)}, bf16[1,2,64,64,64]{4,3,2,1,0:T(8,128)(2,1)}, u32[]{:S(2)}) copy-start(bf16[1,2,64,64,64]{4,3,2,1,0:T(8,128)(2,1)} %copy-done.4) | copy-start | bytes 3145732
  67.9 1.3 copy-start.7
  102.3 2.9 %copy-start.6 = (bf16[1,2,64,64,64]{4,3,2,1,0:T(8,128)(2,1)S(1)}, bf16[1,2,64,64,64]{4,3,2,1,0:T(8,128)(2,1)}, u32[]{:S(2)}) copy-start(bf16[1,2,64,64,64]{4,3,2,1,0:T(8,128)(2,1)} %copy-done.4) | copy-start | bytes 3145732
  106.5 1.3 copy-start.8
  111.4 5.9 %copy-start.3 = (bf16[768,2048]{1,0:T(8,128)(2,1)S(1)}, bf16[768,2048]{1,0:T(8,128)(2,1)}, u32[]{:S(2)}) copy-start(bf16[768,2048]{1,0:T(8,128)(2,1)} %copy-done.2) | copy-start | bytes 9437188
  117.3 14.0 %copy-start.11 = (f32[1,2]{1,0:T(1,128)S(1)}, f32[1,2]{1,0:T(1,128)}, u32[]{:S(2)}) copy-start(f32[1,2]{1,0:T(1,128)} %param.15) | copy-start | bytes 28
  117.3 30.0 %copy-start.1 = (bf16[1,64,2048]{2,1,0:T(8,128)(2,1)S(1)}, bf16[1,64,2048]{2,1,0:T(8,128)(2,1)}, u32[]{:S(2)}) copy-start(bf16[1,64,2048]{2,1,0:T(8,128)(2,1)} %param.10) | copy-start | bytes 786436
